TPU v7x, 256 devices: a whole 4x4x8 slice. The times are simulated.
256 devices in a mesh: lon: 16 (over x, y_lo, core), lat: 16 (over y_hi, z).
Axes of the slice: x: 4, y: 4 (y_hi: 2, y_lo: 2; y = y_hi * 2 + y_lo), z: 8, core: 2. Of those that a mesh axis runs over, the one named last changes fastest.
Arguments:
- height: float32 [3072, 7200], P('lat', 'lon'), may hold values from 0.4 to 1.6
- east_wind: float32 [3072, 7200], P('lat', 'lon'), may hold values from -1.5 to 1.5
- north_wind: float32 [3072, 7200], P('lat', 'lon'), may hold values from -1.5 to 1.5
- cutoffs: int32 [512], replicated, may hold values from 1 to 64
Outputs:
- height_final: float32 [3072, 7200], P('lat', 'lon')
- east_final: float32 [3072, 7200], P('lat', 'lon')
- north_final: float32 [3072, 7200], P('lat', 'lon')
All inputs are finite; a program needn't handle non-finite values.
Results may differ from a plain program's by a relative error of at most 0.0002.
Values sent between devices are 32-bit elements; how exact they have to be, the bound alone decides.
No kernel may reach another device: no remote copies, remote signals or barrier semaphores. Data moves between devices by JAX's collectives and lax.ppermute only.
A program may use at most 128 MiB of HBM per device.

v0:
```python
import math
import jax
import jax.numpy as jnp
from jax import lax
from jax.sharding import PartitionSpec as P

NLON = 7200
LAT_ROWS = 3600
KMAX = 64
STEPS = 2
COURANT = 0.1
OMEGA_RATE = 1.5


def with_halo(value, sides, width, wrap):
    for axis, dim in sides:
        devices, length = (lax.axis_size(axis), value.shape[dim])
        up = [(i, (i + 1) % devices) for i in range(devices if wrap else devices - 1)]
        down = [(j, i) for i, j in up]
        last = lax.slice_in_dim(value, length - width, length, axis=dim)
        first = lax.slice_in_dim(value, 0, width, axis=dim)
        before = lax.ppermute(last, axis, up)
        after = lax.ppermute(first, axis, down)
        value = jnp.concatenate([before, value, after], axis=dim)
    return value


def from_behind(value, axis, by):
    devices = lax.axis_size(axis)
    return lax.ppermute(value, axis, [(i, (i + by) % devices) for i in range(devices)])


def local_table(width):
    waves = jnp.arange(KMAX + 1, dtype=jnp.int32)
    columns = lax.axis_index("lon") * width + jnp.arange(width, dtype=jnp.int32)
    phase = waves[:, None] * columns[None, :] % NLON
    angle = phase.astype(jnp.float32) * (2.0 * math.pi / NLON)
    return jnp.concatenate([jnp.cos(angle), jnp.sin(angle)], axis=0)


def spectral_weights(cut_rows):
    waves = jnp.arange(KMAX + 1, dtype=jnp.int32)
    scale = jnp.where(waves == 0, 1.0 / NLON, 2.0 / NLON).astype(jnp.float32)
    keep = (waves[None, :] <= cut_rows[:, None]).astype(jnp.float32) * scale[None, :]
    return jnp.concatenate([keep, keep], axis=1)


def project(fields, table):
    return jnp.einsum("fnw,kw->fnk", fields, table, precision=lax.Precision.HIGHEST)


def expand(coeffs, table):
    return jnp.einsum("fnk,kw->fnw", coeffs, table, precision=lax.Precision.HIGHEST)


def low_pass(fields, cut_rows, active, table):
    weights = spectral_weights(cut_rows)
    coeffs = lax.psum(project(fields, table), "lon") * weights[None]
    smooth = expand(coeffs, table)
    return jnp.where(active[None, :, None], smooth, fields)


def filter_state(state, cutoffs, table):
    rows_here = state.shape[1]
    lat_count = lax.axis_size("lat")
    lat_index = lax.axis_index("lat")
    filtered_rows = cutoffs.shape[0]
    cut_all = jnp.pad(cutoffs, (0, rows_here * lat_count - filtered_rows))
    global_rows = lat_index * rows_here + jnp.arange(rows_here, dtype=jnp.int32)
    cut_rows = lax.dynamic_slice_in_dim(cut_all, lat_index * rows_here, rows_here, 0)
    return low_pass(state, cut_rows, global_rows < filtered_rows, table)


def tendency(state, cos_all, sinlat, lon_step, lat_step):
    lat_index = lax.axis_index("lat")
    lat_count = lax.axis_size("lat")
    edge_cols = jnp.concatenate([state[:, :, :1], state[:, :, -1:]], axis=2)
    got_cols = with_halo(edge_cols, (("lon", 2),), 1, True)
    west_col = got_cols[:, :, 0:1]
    east_col = got_cols[:, :, 3:4]
    edge_rows = jnp.concatenate([state[:, :1, :], state[:, -1:, :]], axis=1)
    got_rows = with_halo(edge_rows, (("lat", 1),), 1, False)
    flips = jnp.array([1.0, -1.0, -1.0], jnp.float32)
    mirror = from_behind(state[:, 0, :], "lon", lax.axis_size("lon") // 2) * flips[:, None]
    northmost = jnp.where(lat_index == 0, mirror, got_rows[:, 0, :])
    southmost = jnp.where(lat_index == lat_count - 1, state[:, -1, :], got_rows[:, 3, :])
    corner = jnp.zeros((3, 1, 1), jnp.float32)
    top_line = jnp.concatenate([corner, northmost[:, None, :], corner], axis=2)
    bottom_line = jnp.concatenate([corner, southmost[:, None, :], corner], axis=2)
    middle_lines = jnp.concatenate([west_col, state, east_col], axis=2)
    extended = jnp.concatenate([top_line, middle_lines, bottom_line], axis=1)
    east_side = extended[:, 1:-1, 2:]
    west_side = extended[:, 1:-1, :-2]
    north_side = extended[:, :-2, 1:-1]
    south_side = extended[:, 2:, 1:-1]
    cos_north = cos_all[:-2][:, None]
    cos_south = cos_all[2:][:, None]
    coslat = cos_all[1:-1][:, None]

    def zonal_pair(east_value, west_value):
        return (east_value - west_value) * (0.5 / lon_step)

    def north_pair(north_value, south_value):
        return (north_value - south_value) * (0.5 / lat_step)

    height, east, north = (state[0], state[1], state[2])
    inv_cos = 1.0 / coslat
    turning = 2.0 * OMEGA_RATE * sinlat + east * sinlat * inv_cos
    flux_north = north_side[0] * north_side[2] * cos_north
    flux_south = south_side[0] * south_side[2] * cos_south
    rate_height = (
        -(
            zonal_pair(east_side[0] * east_side[1], west_side[0] * west_side[1])
            + north_pair(flux_north, flux_south)
        )
        * inv_cos
    )
    rate_east = (
        -east * zonal_pair(east_side[1], west_side[1]) * inv_cos
        - north * north_pair(north_side[1], south_side[1])
        + turning * north
        - zonal_pair(east_side[0], west_side[0]) * inv_cos
    )
    rate_north = (
        -east * zonal_pair(east_side[2], west_side[2]) * inv_cos
        - north * north_pair(north_side[2], south_side[2])
        - turning * east
        - north_pair(north_side[0], south_side[0])
    )
    return jnp.stack([rate_height, rate_east, rate_north], axis=0)


def shards(height, east_wind, north_wind, cutoffs):
    rows_here = height.shape[0]
    lat_index = lax.axis_index("lat")
    lat_step = math.pi / LAT_ROWS
    lon_step = 2.0 * math.pi / NLON
    time_step = COURANT * lat_step
    first_row = (lat_index * rows_here).astype(jnp.float32)
    index = first_row + jnp.arange(-1, rows_here + 1).astype(jnp.float32)
    cos_all = jnp.abs(jnp.sin((index + 0.5) * lat_step))
    sin_all = jnp.cos((index + 0.5) * lat_step)
    sinlat = sin_all[1:-1][:, None]
    table = local_table(height.shape[1])
    state = jnp.stack([height, east_wind, north_wind], axis=0)
    for step_index in range(STEPS):
        rates = tendency(state, cos_all, sinlat, lon_step, lat_step)
        middle = state + 0.5 * time_step * rates
        rates = tendency(middle, cos_all, sinlat, lon_step, lat_step)
        advanced = state + time_step * rates
        state = filter_state(advanced, cutoffs, table)
    return (state[0], state[1], state[2])


def solution(mesh):
    placed = (P("lat", "lon"), P("lat", "lon"), P("lat", "lon"), P())
    return jax.shard_map(
        shards,
        mesh=mesh,
        in_specs=placed,
        out_specs=(P("lat", "lon"), P("lat", "lon"), P("lat", "lon")),
        check_vma=False,
    )
```

profile of v0, /device:TPU:16, one launch (start us, length us, event | category | flops | bytes accessed | tf_op | source)
XLA Modules:
  0.0 351.3 jit_solution(10091914671788850582)
XLA Ops:
  7.2 1.3 pad_maximum_fusion
  9.4 2.9 collective-permute-start
  12.9 7.8 %collective-permute-start.4 = (f32[3,1,450]{2,1,0:T(1,128)}, f32[3,1,450]{2,1,0:T(1,128)}, u32[]{:S(2)}, u32[]{:S(2)}) collective-permute-start(f32[3,1,450]{2,1,0:T(1,128)} %get-tuple-element.26), channel_id=1, source_target_pairs={{1,0},{2,1},{3,2},{4,3},{5,4},{6,5},{7,6},{8,7},{9,8},{10,9},{11,1... | collective-permute-start | bytes 16208 | tf_op jit(solution)/shard_map/ppermute | solution.py:23
  20.7 1.3 copy.94
  23.4 1.9 collective-permute-start.3
  28.5 4.4 %collective-permute-done.3 = f32[3,1,450]{2,0,1:T(4,128)} collective-permute-done((f32[3,1,450]{2,0,1:T(4,128)}, f32[3,1,450]{2,0,1:T(4,128)}, u32[]{:S(2)}, u32[]{:S(2)}) %collective-permute-start.3) | collective-permute-done | bytes 5432 | tf_op jit(solution)/shard_map/ppermute | solution.py:22
  36.4 3.3 collective-permute-start.9
  39.6 2.8 collective-permute-start.7
  42.5 2.6 collective-permute-start.8
  45.2 2.5 collective-permute-start.5
  47.7 3.9 %collective-permute-done.8 = f32[3,1,450]{2,0,1:T(4,128)S(1)} collective-permute-done((f32[3,1,450]{2,0,1:T(4,128)S(1)}, f32[3,1,450]{2,0,1:T(4,128)S(1)}, u32[]{:S(2)}, u32[]{:S(2)}) %collective-permute-start.8) | collective-permute-done | bytes 5432 | tf_op jit(solution)/shard_map/ppermute | solution.py:22
  51.9 4.0 %collective-permute-done.6 = f32[3,192,1]{2,1,0:T(8,128)S(1)} collective-permute-done((f32[3,192,1]{2,1,0:T(8,128)S(1)}, f32[3,192,1]{2,1,0:T(8,128)S(1)}, u32[]{:S(2)}, u32[]{:S(2)}) %collective-permute-start.6) | collective-permute-done | bytes 2336 | tf_op jit(solution)/shard_map/ppermute | solution.py:22
  57.6 1.5 fusion.50
  59.0 3.2 fusion.89
  62.6 114.6 %all-reduce.4.cloned.1.call-done = f32[3,192,130]{1,2,0:T(8,128)} async-done(((f32[3,192,130]{1,2,0:T(8,128)}), f32[3,192,130]{1,2,0:T(8,128)}) %all-reduce.4.cloned.1.call-update) | async-done | bytes 299536 | tf_op jit(solution)/shard_map/psum | solution.py:58
  177.2 2.7 convolution_select_fusion.1
  180.0 5.2 %collective-permute-start.14 = (f32[3,1,450]{2,0,1:T(4,128)S(1)}, f32[3,1,450]{2,0,1:T(4,128)S(1)}, u32[]{:S(2)}, u32[]{:S(2)}) collective-permute-start(f32[3,1,450]{2,0,1:T(4,128)S(1)} %copy.96), channel_id=1, source_target_pairs={{1,0},{2,1},{3,2},{4,3},{5,4},{6,5},{7,6},{8,7},{9,8},{10,9},{11,1... | collective-permute-start | bytes 16208 | tf_op jit(solution)/shard_map/ppermute | solution.py:23
  185.3 1.2 collective-permute-done.14
  186.5 2.5 collective-permute-start.13
  190.4 5.5 %collective-permute-done.13 = f32[3,1,450]{2,0,1:T(4,128)S(1)} collective-permute-done((f32[3,1,450]{2,0,1:T(4,128)S(1)}, f32[3,1,450]{2,0,1:T(4,128)S(1)}, u32[]{:S(2)}, u32[]{:S(2)}) %collective-permute-start.13) | collective-permute-done | bytes 5432 | tf_op jit(solution)/shard_map/ppermute | solution.py:22
  196.2 1.4 collective-permute-done.11
  200.2 7.2 %collective-permute-start.19 = (f32[3,1,450]{2,0,1:T(4,128)S(1)}, f32[3,1,450]{2,0,1:T(4,128)S(1)}, u32[]{:S(2)}, u32[]{:S(2)}) collective-permute-start(f32[3,1,450]{2,0,1:T(4,128)S(1)} %copy.95), channel_id=1, source_target_pairs={{1,0},{2,1},{3,2},{4,3},{5,4},{6,5},{7,6},{8,7},{9,8},{10,9},{11,1... | collective-permute-start | bytes 16208 | tf_op jit(solution)/shard_map/ppermute | solution.py:23
  207.5 0.9 collective-permute-start.17
  208.8 1.9 collective-permute-start.18
  211.5 1.2 collective-permute-done.17
  212.7 5.6 %collective-permute-done.18 = f32[3,1,450]{2,0,1:T(4,128)S(1)} collective-permute-done((f32[3,1,450]{2,0,1:T(4,128)S(1)}, f32[3,1,450]{2,0,1:T(4,128)S(1)}, u32[]{:S(2)}, u32[]{:S(2)}) %collective-permute-start.18) | collective-permute-done | bytes 5432 | tf_op jit(solution)/shard_map/ppermute | solution.py:22
  218.5 1.1 collective-permute-done.16
  219.6 0.8 fusion.75
  221.9 2.2 fusion.88
  224.1 116.8 %all-reduce.6.cloned.1.call-done = f32[3,192,130]{1,2,0:T(8,128)} async-done(((f32[3,192,130]{1,2,0:T(8,128)}), f32[3,192,130]{1,2,0:T(8,128)}) %all-reduce.6.cloned.1.call-update) | async-done | bytes 299536 | tf_op jit(solution)/shard_map/psum | solution.py:58
  340.9 2.5 convolution_select_fusion
  343.4 1.0 slice_bitcast_fusion
  (103 shorter events, 18.9 us)
Async XLA Ops:
  7.2 170.1 %all-reduce.4.cloned.1.call-start = ((), (), s32[]{:S(2)}) async-start(), calls=%async_computation | async-start | bytes 835584 | tf_op jit(solution)/shard_map/psum | solution.py:58
  8.5 19.4 %copy-start = (f32[192,450]{1,0:T(8,128)S(1)}, f32[192,450]{1,0:T(8,128)}, u32[]{:S(2)}) copy-start(f32[192,450]{1,0:T(8,128)} %param.10) | copy-start | bytes 1036804
  8.6 19.4 %copy-start.1 = (f32[192,450]{1,0:T(8,128)S(1)}, f32[192,450]{1,0:T(8,128)}, u32[]{:S(2)}) copy-start(f32[192,450]{1,0:T(8,128)} %param.9) | copy-start | bytes 1036804
  8.6 19.4 %copy-start.2 = (f32[192,450]{1,0:T(8,128)S(1)}, f32[192,450]{1,0:T(8,128)}, u32[]{:S(2)}) copy-start(f32[192,450]{1,0:T(8,128)} %param.8) | copy-start | bytes 1036804
  9.4 18.6 %collective-permute-start = (f32[3,192,1]{2,1,0:T(8,128)}, f32[3,192,1]{2,1,0:T(8,128)S(1)}, u32[]{:S(2)}, u32[]{:S(2)}) collective-permute-start(f32[3,192,1]{2,1,0:T(8,128)} %get-tuple-element.29), channel_id=1, source_target_pairs={{16,0},{32,16},{48,32},{64,48},{80,64},{96,80},{112,96},{128,112},... | collective-permute-start | bytes 6920 | tf_op jit(solution)/shard_map/ppermute | solution.py:23
  12.3 15.7 %collective-permute-start.1 = (f32[3,192,1]{2,1,0:T(8,128)S(1)}, f32[3,192,1]{2,1,0:T(8,128)S(1)}, u32[]{:S(2)}, u32[]{:S(2)}) collective-permute-start(f32[3,192,1]{2,1,0:T(8,128)S(1)} %get-tuple-element.30), channel_id=1, source_target_pairs={{0,16},{16,32},{32,48},{48,64},{64,80},{80,96},{96,112},{112,128},... | collective-permute-start | bytes 6920 | tf_op jit(solution)/shard_map/ppermute | solution.py:22
  12.9 20.9 %collective-permute-start.4 = (f32[3,1,450]{2,1,0:T(1,128)}, f32[3,1,450]{2,1,0:T(1,128)}, u32[]{:S(2)}, u32[]{:S(2)}) collective-permute-start(f32[3,1,450]{2,1,0:T(1,128)} %get-tuple-element.26), channel_id=1, source_target_pairs={{1,0},{2,1},{3,2},{4,3},{5,4},{6,5},{7,6},{8,7},{9,8},{10,9},{11,1... | collective-permute-start | bytes 16208 | tf_op jit(solution)/shard_map/ppermute | solution.py:23
  22.0 6.5 %collective-permute-start.2 = (f32[3,450]{1,0:T(4,128)}, f32[3,450]{1,0:T(4,128)}, u32[]{:S(2)}, u32[]{:S(2)}) collective-permute-start(f32[3,450]{1,0:T(4,128)} %bitcast.93), channel_id=1, source_target_pairs={{0,128},{16,144},{32,160},{48,176},{64,192},{80,208},{96,224},{112... | collective-permute-start | bytes 16208 | tf_op jit(solution)/shard_map/ppermute | solution.py:30
  23.4 9.5 %collective-permute-start.3 = (f32[3,1,450]{2,0,1:T(4,128)}, f32[3,1,450]{2,0,1:T(4,128)}, u32[]{:S(2)}, u32[]{:S(2)}) collective-permute-start(f32[3,1,450]{2,0,1:T(4,128)} %copy.74), channel_id=1, source_target_pairs={{0,1},{1,2},{2,3},{3,4},{4,5},{5,6},{6,7},{7,8},{8,9},{9,10},{10,1... | collective-permute-start | bytes 16208 | tf_op jit(solution)/shard_map/ppermute | solution.py:22
  28.0 4.9 %copy-start.8 = (f32[3]{0:T(128)S(1)}, f32[3]{0:T(128)}, u32[]{:S(2)}) copy-start(f32[3]{0:T(128)} %constant.57.clone) | copy-start | bytes 40
  28.0 6.5 %copy-start.4 = (f32[192]{0:T(256)S(1)}, f32[192]{0:T(256)}, u32[]{:S(2)}) copy-start(f32[192]{0:T(256)} %get-tuple-element.53) | copy-start | bytes 2308
  28.0 6.6 %copy-start.6 = (f32[192]{0:T(256)S(1)}, f32[192]{0:T(256)}, u32[]{:S(2)}) copy-start(f32[192]{0:T(256)} %get-tuple-element.54) | copy-start | bytes 2308
  36.4 6.1 %collective-permute-start.9 = (f32[3,1,450]{2,0,1:T(4,128)S(1)}, f32[3,1,450]{2,0,1:T(4,128)S(1)}, u32[]{:S(2)}, u32[]{:S(2)}) collective-permute-start(f32[3,1,450]{2,0,1:T(4,128)S(1)} %copy.97), channel_id=1, source_target_pairs={{1,0},{2,1},{3,2},{4,3},{5,4},{6,5},{7,6},{8,7},{9,8},{10,9},{11,1... | collective-permute-start | bytes 16208 | tf_op jit(solution)/shard_map/ppermute | solution.py:23
  39.6 8.1 %collective-permute-start.7 = (f32[3,450]{1,0:T(4,128)S(1)}, f32[3,450]{1,0:T(4,128)S(1)}, u32[]{:S(2)}, u32[]{:S(2)}) collective-permute-start(f32[3,450]{1,0:T(4,128)S(1)} %bitcast.115), channel_id=1, source_target_pairs={{0,128},{16,144},{32,160},{48,176},{64,192},{80,208},{96,224},{112... | collective-permute-start | bytes 16208 | tf_op jit(solution)/shard_map/ppermute | solution.py:30
  42.5 9.2 %collective-permute-start.8 = (f32[3,1,450]{2,0,1:T(4,128)S(1)}, f32[3,1,450]{2,0,1:T(4,128)S(1)}, u32[]{:S(2)}, u32[]{:S(2)}) collective-permute-start(f32[3,1,450]{2,0,1:T(4,128)S(1)} %get-tuple-element.40), channel_id=1, source_target_pairs={{0,1},{1,2},{2,3},{3,4},{4,5},{5,6},{6,7},{7,8},{8,9},{9,10},{10,1... | collective-permute-start | bytes 16208 | tf_op jit(solution)/shard_map/ppermute | solution.py:22
  45.2 6.7 %collective-permute-start.5 = (f32[3,192,1]{2,1,0:T(8,128)S(1)}, f32[3,192,1]{2,1,0:T(8,128)S(1)}, u32[]{:S(2)}, u32[]{:S(2)}) collective-permute-start(f32[3,192,1]{2,1,0:T(8,128)S(1)} %get-tuple-element.23), channel_id=1, source_target_pairs={{16,0},{32,16},{48,32},{64,48},{80,64},{96,80},{112,96},{128,112},... | collective-permute-start | bytes 6920 | tf_op jit(solution)/shard_map/ppermute | solution.py:23
  47.7 8.3 %collective-permute-start.6 = (f32[3,192,1]{2,1,0:T(8,128)S(1)}, f32[3,192,1]{2,1,0:T(8,128)S(1)}, u32[]{:S(2)}, u32[]{:S(2)}) collective-permute-start(f32[3,192,1]{2,1,0:T(8,128)S(1)} %get-tuple-element.24), channel_id=1, source_target_pairs={{0,16},{16,32},{32,48},{48,64},{64,80},{80,96},{96,112},{112,128},... | collective-permute-start | bytes 6920 | tf_op jit(solution)/shard_map/ppermute | solution.py:22
  59.0 3.5 copy-start.11
  62.2 278.7 %all-reduce.6.cloned.1.call-start = ((), (), s32[]{:S(2)}) async-start(), calls=%async_computation.1 | async-start | bytes 835584 | tf_op jit(solution)/shard_map/psum | solution.py:58
  179.9 16.0 %copy-start.9 = (f32[3]{0:T(128)S(1)}, f32[3]{0:T(128)}, u32[]{:S(2)}) copy-start(f32[3]{0:T(128)} %constant.57.clone) | copy-start | bytes 40
  180.0 17.7 %copy-start.5 = (f32[192]{0:T(256)S(1)}, f32[192]{0:T(256)}, u32[]{:S(2)}) copy-start(f32[192]{0:T(256)} %get-tuple-element.53) | copy-start | bytes 2308
  180.0 17.6 %copy-start.7 = (f32[192]{0:T(256)S(1)}, f32[192]{0:T(256)}, u32[]{:S(2)}) copy-start(f32[192]{0:T(256)} %get-tuple-element.54) | copy-start | bytes 2308
  180.0 6.5 %collective-permute-start.14 = (f32[3,1,450]{2,0,1:T(4,128)S(1)}, f32[3,1,450]{2,0,1:T(4,128)S(1)}, u32[]{:S(2)}, u32[]{:S(2)}) collective-permute-start(f32[3,1,450]{2,0,1:T(4,128)S(1)} %copy.96), channel_id=1, source_target_pairs={{1,0},{2,1},{3,2},{4,3},{5,4},{6,5},{7,6},{8,7},{9,8},{10,9},{11,1... | collective-permute-start | bytes 16208 | tf_op jit(solution)/shard_map/ppermute | solution.py:23
  185.2 5.2 %collective-permute-start.12 = (f32[3,450]{1,0:T(4,128)S(1)}, f32[3,450]{1,0:T(4,128)S(1)}, u32[]{:S(2)}, u32[]{:S(2)}) collective-permute-start(f32[3,450]{1,0:T(4,128)S(1)} %bitcast.117), channel_id=1, source_target_pairs={{0,128},{16,144},{32,160},{48,176},{64,192},{80,208},{96,224},{112... | collective-permute-start | bytes 16208 | tf_op jit(solution)/shard_map/ppermute | solution.py:30
  186.5 9.4 %collective-permute-start.13 = (f32[3,1,450]{2,0,1:T(4,128)S(1)}, f32[3,1,450]{2,0,1:T(4,128)S(1)}, u32[]{:S(2)}, u32[]{:S(2)}) collective-permute-start(f32[3,1,450]{2,0,1:T(4,128)S(1)} %get-tuple-element.36), channel_id=1, source_target_pairs={{0,1},{1,2},{2,3},{3,4},{4,5},{5,6},{6,7},{7,8},{8,9},{9,10},{10,1... | collective-permute-start | bytes 16208 | tf_op jit(solution)/shard_map/ppermute | solution.py:22
  189.2 7.0 %collective-permute-start.10 = (f32[3,192,1]{2,1,0:T(8,128)S(1)}, f32[3,192,1]{2,1,0:T(8,128)S(1)}, u32[]{:S(2)}, u32[]{:S(2)}) collective-permute-start(f32[3,192,1]{2,1,0:T(8,128)S(1)} %get-tuple-element.19), channel_id=1, source_target_pairs={{16,0},{32,16},{48,32},{64,48},{80,64},{96,80},{112,96},{128,112},... | collective-permute-start | bytes 6920 | tf_op jit(solution)/shard_map/ppermute | solution.py:23
  189.3 8.3 %collective-permute-start.11 = (f32[3,192,1]{2,1,0:T(8,128)S(1)}, f32[3,192,1]{2,1,0:T(8,128)S(1)}, u32[]{:S(2)}, u32[]{:S(2)}) collective-permute-start(f32[3,192,1]{2,1,0:T(8,128)S(1)} %get-tuple-element.20), channel_id=1, source_target_pairs={{0,16},{16,32},{32,48},{48,64},{64,80},{80,96},{96,112},{112,128},... | collective-permute-start | bytes 6920 | tf_op jit(solution)/shard_map/ppermute | solution.py:22
  200.2 8.6 %collective-permute-start.19 = (f32[3,1,450]{2,0,1:T(4,128)S(1)}, f32[3,1,450]{2,0,1:T(4,128)S(1)}, u32[]{:S(2)}, u32[]{:S(2)}) collective-permute-start(f32[3,1,450]{2,0,1:T(4,128)S(1)} %copy.95), channel_id=1, source_target_pairs={{1,0},{2,1},{3,2},{4,3},{5,4},{6,5},{7,6},{8,7},{9,8},{10,9},{11,1... | collective-permute-start | bytes 16208 | tf_op jit(solution)/shard_map/ppermute | solution.py:23
  207.5 5.2 %collective-permute-start.17 = (f32[3,450]{1,0:T(4,128)S(1)}, f32[3,450]{1,0:T(4,128)S(1)}, u32[]{:S(2)}, u32[]{:S(2)}) collective-permute-start(f32[3,450]{1,0:T(4,128)S(1)} %bitcast.116), channel_id=1, source_target_pairs={{0,128},{16,144},{32,160},{48,176},{64,192},{80,208},{96,224},{112... | collective-permute-start | bytes 16208 | tf_op jit(solution)/shard_map/ppermute | solution.py:30
  208.8 9.5 %collective-permute-start.18 = (f32[3,1,450]{2,0,1:T(4,128)S(1)}, f32[3,1,450]{2,0,1:T(4,128)S(1)}, u32[]{:S(2)}, u32[]{:S(2)}) collective-permute-start(f32[3,1,450]{2,0,1:T(4,128)S(1)} %get-tuple-element.32), channel_id=1, source_target_pairs={{0,1},{1,2},{2,3},{3,4},{4,5},{5,6},{6,7},{7,8},{8,9},{9,10},{10,1... | collective-permute-start | bytes 16208 | tf_op jit(solution)/shard_map/ppermute | solution.py:22
  210.9 7.6 %collective-permute-start.15 = (f32[3,192,1]{2,1,0:T(8,128)S(1)}, f32[3,192,1]{2,1,0:T(8,128)S(1)}, u32[]{:S(2)}, u32[]{:S(2)}) collective-permute-start(f32[3,192,1]{2,1,0:T(8,128)S(1)} %get-tuple-element.15), channel_id=1, source_target_pairs={{16,0},{32,16},{48,32},{64,48},{80,64},{96,80},{112,96},{128,112},... | collective-permute-start | bytes 6920 | tf_op jit(solution)/shard_map/ppermute | solution.py:23
  211.2 8.4 %collective-permute-start.16 = (f32[3,192,1]{2,1,0:T(8,128)S(1)}, f32[3,192,1]{2,1,0:T(8,128)S(1)}, u32[]{:S(2)}, u32[]{:S(2)}) collective-permute-start(f32[3,192,1]{2,1,0:T(8,128)S(1)} %get-tuple-element.16), channel_id=1, source_target_pairs={{0,16},{16,32},{32,48},{48,64},{64,80},{80,96},{96,112},{112,128},... | collective-permute-start | bytes 6920 | tf_op jit(solution)/shard_map/ppermute | solution.py:22
  (2 other events, 4.9 us)
Sparse Core Ops, SparseCore 0:
  62.4 114.8 all-reduce.3
  224.2 116.6 all-reduce.5
where the time goes:
time: 352 us; the launch traced here: 351 us
  waiting for transfers between devices  261 us (74%)
  starting transfers between devices  43.8 us (12%)
  other arithmetic  15.6 us (4%)
  between operations  14.5 us (4%)
  matrix products  10.5 us (3%)
  local copies, waits for them, and re-layouts  5.62 us (2%)
    psum x2, waiting for transfers between devices, low_pass(): coeffs = lax.psum(project(fields, table), 'lon') * weights[None]  231 us
    ppermute x8, starting transfers between devices, with_halo(): after = lax.ppermute(first, axis, down)  29.4 us
    ppermute x8, waiting for transfers between devices, with_halo(): before = lax.ppermute(last, axis, up)  26 us
    ppermute x8, starting transfers between devices, with_halo(): before = lax.ppermute(last, axis, up)  9.59 us
  transfers between devices with their start and end apart: 22, of which 14 were waited for; matrix products, arithmetic and copies ran while one was open for 2% of the time, Pallas kernels for 0%

commit v1 on v0

--- a/solution.py
+++ b/solution.py
@@ -55,7 +55,9 @@
 
 def low_pass(fields, cut_rows, active, table):
     weights = spectral_weights(cut_rows)
-    coeffs = lax.psum(project(fields, table), "lon") * weights[None]
+    coeffs = (
+        jnp.sum(lax.all_gather(project(fields, table), axis_name="lon"), axis=0) * weights[None]
+    )
     smooth = expand(coeffs, table)
     return jnp.where(active[None, :, None], smooth, fields)
 

time: 352 us -> 227 us (0.64)
  waiting for transfers between devices: 261 us -> 127 us
  other arithmetic: 15.6 us -> 22.3 us
    psum x2 -> x0, waiting for transfers between devices: 231 us -> none  [low_pass(): coeffs = lax.psum(project(fields, table), 'lon') * weights[None]]
    all_gather x0 -> x2, waiting for transfers between devices: none -> 94 us  [low_pass(): lax.all_gather(project(fields, table), axis_name='lon')]
    reduce_sum x0 -> x2, other arithmetic: none -> 7.54 us  [low_pass(): jnp.sum(lax.all_gather(project(fields, table), axis_name='lon'), axis=0)]
  transfers between devices with their start and end apart: 22 -> 22, of which waited for: 14 -> 14; matrix products, arithmetic and copies ran while one was open for 2% -> 3% of each run, Pallas kernels for 0% -> 0%
where the time goes in v1:
time: 227 us; the launch traced here: 225 us
  waiting for transfers between devices  127 us (56%)
  starting transfers between devices  45.5 us (20%)
  other arithmetic  22.3 us (10%)
  between operations  14.7 us (6%)
  matrix products  9.67 us (4%)
  local copies, waits for them, and re-layouts  5.42 us (2%)
    all_gather x2, waiting for transfers between devices, low_pass(): lax.all_gather(project(fields, table), axis_name='lon')  94 us
    ppermute x8, starting transfers between devices, with_halo(): after = lax.ppermute(first, axis, down)  30.7 us
    ppermute x8, waiting for transfers between devices, with_halo(): before = lax.ppermute(last, axis, up)  25.5 us
    ppermute x8, starting transfers between devices, with_halo(): before = lax.ppermute(last, axis, up)  8.29 us
    reduce_sum x2, other arithmetic, low_pass(): jnp.sum(lax.all_gather(project(fields, table), axis_name='lon'), axis=0)  7.54 us
    ppermute x4, starting transfers between devices, from_behind(): lax.ppermute(value, axis, [(i, (i + by) % devices) for i in range(devices)])  6.2 us
    dot_general x2, matrix products, expand(): jnp.einsum('fnk,kw->fnw', coeffs, table, precision=lax.Precision.HIGHEST)  5.32 us
  transfers between devices with their start and end apart: 22, of which 14 were waited for; matrix products, arithmetic and copies ran while one was open for 3% of the time, Pallas kernels for 0%

profile of v1, /device:TPU:16, one launch (start us, length us, event | category | flops | bytes accessed | tf_op | source)
XLA Modules:
  0.0 224.8 jit_solution(17507982511708236918)
XLA Ops:
  7.2 1.3 pad_maximum_fusion
  9.2 7.5 %collective-permute-start.4 = (f32[3,1,450]{2,1,0:T(1,128)}, f32[3,1,450]{2,1,0:T(1,128)}, u32[]{:S(2)}, u32[]{:S(2)}) collective-permute-start(f32[3,1,450]{2,1,0:T(1,128)} %get-tuple-element.26), channel_id=1, source_target_pairs={{1,0},{2,1},{3,2},{4,3},{5,4},{6,5},{7,6},{8,7},{9,8},{10,9},{11,1... | collective-permute-start | bytes 16208 | tf_op jit(solution)/shard_map/ppermute | solution.py:23
  16.7 1.3 copy.126
  18.0 3.0 %collective-permute-start.2 = (f32[3,450]{1,0:T(4,128)}, f32[3,450]{1,0:T(4,128)}, u32[]{:S(2)}, u32[]{:S(2)}) collective-permute-start(f32[3,450]{1,0:T(4,128)} %bitcast.95), channel_id=1, source_target_pairs={{0,128},{16,144},{32,160},{48,176},{64,192},{80,208},{96,224},{112... | collective-permute-start | bytes 16208 | tf_op jit(solution)/shard_map/ppermute | solution.py:30
  21.6 1.9 collective-permute-start.3
  23.7 1.7 collective-permute-start
  26.8 2.9 %collective-permute-done = f32[3,192,1]{2,1,0:T(8,128)S(1)} collective-permute-done((f32[3,192,1]{2,1,0:T(8,128)S(1)}, f32[3,192,1]{2,1,0:T(8,128)S(1)}, u32[]{:S(2)}, u32[]{:S(2)}) %collective-permute-start) | collective-permute-done | bytes 2336 | tf_op jit(solution)/shard_map/ppermute | solution.py:23
  29.7 4.1 %collective-permute-done.1 = f32[3,192,1]{2,1,0:T(8,128)S(1)} collective-permute-done((f32[3,192,1]{2,1,0:T(8,128)S(1)}, f32[3,192,1]{2,1,0:T(8,128)S(1)}, u32[]{:S(2)}, u32[]{:S(2)}) %collective-permute-start.1) | collective-permute-done | bytes 2336 | tf_op jit(solution)/shard_map/ppermute | solution.py:22
  37.8 6.7 %collective-permute-start.9 = (f32[3,1,450]{2,0,1:T(4,128)S(1)}, f32[3,1,450]{2,0,1:T(4,128)S(1)}, u32[]{:S(2)}, u32[]{:S(2)}) collective-permute-start(f32[3,1,450]{2,0,1:T(4,128)S(1)} %copy.129), channel_id=1, source_target_pairs={{1,0},{2,1},{3,2},{4,3},{5,4},{6,5},{7,6},{8,7},{9,8},{10,9},{11,1... | collective-permute-start | bytes 16208 | tf_op jit(solution)/shard_map/ppermute | solution.py:23
  45.8 1.9 collective-permute-start.8
  48.5 1.9 collective-permute-done.7
  50.4 5.1 %collective-permute-done.8 = f32[3,1,450]{2,0,1:T(4,128)S(1)} collective-permute-done((f32[3,1,450]{2,0,1:T(4,128)S(1)}, f32[3,1,450]{2,0,1:T(4,128)S(1)}, u32[]{:S(2)}, u32[]{:S(2)}) %collective-permute-start.8) | collective-permute-done | bytes 5432 | tf_op jit(solution)/shard_map/ppermute | solution.py:22
  55.7 1.5 collective-permute-done.6
  60.3 2.2 fusion.89
  62.9 46.6 %all-gather.5.cloned.1.call-done = f32[48,192,130]{1,2,0:T(8,128)} async-done(((f32[3,192,130]{1,2,0:T(8,128)}), f32[48,192,130]{1,2,0:T(8,128)}) %all-gather.5.cloned.1.call-update) | async-done | bytes 4792336 | tf_op jit(solution)/shard_map/all_gather | solution.py:59
  109.5 3.4 %reduce_sum.18 = f32[3,192,130]{1,2,0:T(8,128)S(1)} reduce(f32[16,3,192,130]{2,3,1,0:T(8,128)} %bitcast.117, f32[]{:T(128)} %constant.25.clone.1), dimensions={0}, to_apply=%region_0.1 | reduce | flops 1123200 | bytes 5091844 | tf_op jit(solution)/shard_map/reduce_sum | solution.py:59
  113.0 2.7 %convolution_select_fusion.1 = f32[3,192,450]{2,1,0:T(8,128)S(1)} fusion(pred[192]{0:T(512)(128)(4,1)S(1)} %add_compare_fusion, f32[3,192,130]{1,2,0:T(8,128)S(1)} %reduce_sum.18, f32[192,130]{0,1:T(8,128)S(1)} %pad_maximum_fusion.51, f32[65,450]{1,0:T(8,128)S(1)} %get-tuple-element.50, f32[65,450]{1,0:T(8,128)S(1)} %get-tuple-element.49, ...), kind=kOutput, calls=%fused_computation.13 | convolution fusion | flops 406299776 | bytes 3743952 | tf_op jit(solution)/shard_map/fnk,kw->fnw/dot_general | solution.py:53
  115.7 5.3 %collective-permute-start.14 = (f32[3,1,450]{2,0,1:T(4,128)S(1)}, f32[3,1,450]{2,0,1:T(4,128)S(1)}, u32[]{:S(2)}, u32[]{:S(2)}) collective-permute-start(f32[3,1,450]{2,0,1:T(4,128)S(1)} %copy.128), channel_id=1, source_target_pairs={{1,0},{2,1},{3,2},{4,3},{5,4},{6,5},{7,6},{8,7},{9,8},{10,9},{11,1... | collective-permute-start | bytes 16208 | tf_op jit(solution)/shard_map/ppermute | solution.py:23
  121.0 2.7 %collective-permute-start.12 = (f32[3,450]{1,0:T(4,128)S(1)}, f32[3,450]{1,0:T(4,128)S(1)}, u32[]{:S(2)}, u32[]{:S(2)}) collective-permute-start(f32[3,450]{1,0:T(4,128)S(1)} %bitcast.121), channel_id=1, source_target_pairs={{0,128},{16,144},{32,160},{48,176},{64,192},{80,208},{96,224},{112... | collective-permute-start | bytes 16208 | tf_op jit(solution)/shard_map/ppermute | solution.py:30
  123.7 1.9 collective-permute-start.13
  125.8 2.4 %collective-permute-start.10 = (f32[3,192,1]{2,1,0:T(8,128)S(1)}, f32[3,192,1]{2,1,0:T(8,128)S(1)}, u32[]{:S(2)}, u32[]{:S(2)}) collective-permute-start(f32[3,192,1]{2,1,0:T(8,128)S(1)} %get-tuple-element.19), channel_id=1, source_target_pairs={{16,0},{32,16},{48,32},{64,48},{80,64},{96,80},{112,96},{128,112},... | collective-permute-start | bytes 6920 | tf_op jit(solution)/shard_map/ppermute | solution.py:23
  128.2 4.8 %collective-permute-done.13 = f32[3,1,450]{2,0,1:T(4,128)S(1)} collective-permute-done((f32[3,1,450]{2,0,1:T(4,128)S(1)}, f32[3,1,450]{2,0,1:T(4,128)S(1)}, u32[]{:S(2)}, u32[]{:S(2)}) %collective-permute-start.13) | collective-permute-done | bytes 5432 | tf_op jit(solution)/shard_map/ppermute | solution.py:22
  133.2 3.3 %collective-permute-done.11 = f32[3,192,1]{2,1,0:T(8,128)S(1)} collective-permute-done((f32[3,192,1]{2,1,0:T(8,128)S(1)}, f32[3,192,1]{2,1,0:T(8,128)S(1)}, u32[]{:S(2)}, u32[]{:S(2)}) %collective-permute-start.11) | collective-permute-done | bytes 2336 | tf_op jit(solution)/shard_map/ppermute | solution.py:22
  139.1 6.7 %collective-permute-start.19 = (f32[3,1,450]{2,0,1:T(4,128)S(1)}, f32[3,1,450]{2,0,1:T(4,128)S(1)}, u32[]{:S(2)}, u32[]{:S(2)}) collective-permute-start(f32[3,1,450]{2,0,1:T(4,128)S(1)} %copy.127), channel_id=1, source_target_pairs={{1,0},{2,1},{3,2},{4,3},{5,4},{6,5},{7,6},{8,7},{9,8},{10,9},{11,1... | collective-permute-start | bytes 16208 | tf_op jit(solution)/shard_map/ppermute | solution.py:23
  145.8 1.2 collective-permute-done.19
  147.1 1.9 collective-permute-start.18
  149.7 1.2 collective-permute-done.17
  151.0 5.5 %collective-permute-done.18 = f32[3,1,450]{2,0,1:T(4,128)S(1)} collective-permute-done((f32[3,1,450]{2,0,1:T(4,128)S(1)}, f32[3,1,450]{2,0,1:T(4,128)S(1)}, u32[]{:S(2)}, u32[]{:S(2)}) %collective-permute-start.18) | collective-permute-done | bytes 5432 | tf_op jit(solution)/shard_map/ppermute | solution.py:22
  160.5 2.2 fusion.88
  162.7 47.5 %all-gather.7.cloned.1.call-done = f32[48,192,130]{1,2,0:T(8,128)} async-done(((f32[3,192,130]{1,2,0:T(8,128)}), f32[48,192,130]{1,2,0:T(8,128)}) %all-gather.7.cloned.1.call-update) | async-done | bytes 4792336 | tf_op jit(solution)/shard_map/all_gather | solution.py:59
  210.1 4.1 %reduce_sum.19 = f32[3,192,130]{1,2,0:T(8,128)} reduce(f32[16,3,192,130]{2,3,1,0:T(8,128)} %bitcast.118, f32[]{:T(128)} %constant.25.clone.1), dimensions={0}, to_apply=%region_1.2 | reduce | flops 1123200 | bytes 5091844 | tf_op jit(solution)/shard_map/reduce_sum | solution.py:59
  214.3 2.6 %convolution_select_fusion = f32[3,192,450]{2,1,0:T(8,128)S(1)} fusion(pred[192]{0:T(512)(128)(4,1)S(1)} %copy-done.20, f32[3,192,130]{1,2,0:T(8,128)} %reduce_sum.19, f32[192,130]{0,1:T(8,128)} %copy-done.7, f32[65,450]{1,0:T(8,128)} %copy-done.5, f32[65,450]{1,0:T(8,128)} %copy-done.3, f32[3,192,450]{2,1,0:T(8,128)S(1)} %convolution_select_fusion.1, ...), kind=kOutput, calls=%fused_computation.12 | convolution fusion | flops 405781376 | bytes 3743952 | tf_op jit(solution)/shard_map/fnk,kw->fnw/dot_general | solution.py:53
  (123 shorter events, 21.1 us)
Async XLA Ops:
  7.2 102.4 %all-gather.5.cloned.1.call-start = ((), (), s32[]{:S(2)}) async-start(), calls=%async_computation | async-start | bytes 7102464 | tf_op jit(solution)/shard_map/all_gather | solution.py:59
  8.5 25.3 %copy-start = (f32[192,450]{1,0:T(8,128)S(1)}, f32[192,450]{1,0:T(8,128)}, u32[]{:S(2)}) copy-start(f32[192,450]{1,0:T(8,128)} %param.10) | copy-start | bytes 1036804
  8.6 25.3 %copy-start.1 = (f32[192,450]{1,0:T(8,128)S(1)}, f32[192,450]{1,0:T(8,128)}, u32[]{:S(2)}) copy-start(f32[192,450]{1,0:T(8,128)} %param.9) | copy-start | bytes 1036804
  8.6 25.2 %copy-start.2 = (f32[192,450]{1,0:T(8,128)S(1)}, f32[192,450]{1,0:T(8,128)}, u32[]{:S(2)}) copy-start(f32[192,450]{1,0:T(8,128)} %param.8) | copy-start | bytes 1036804
  9.2 26.1 %collective-permute-start.4 = (f32[3,1,450]{2,1,0:T(1,128)}, f32[3,1,450]{2,1,0:T(1,128)}, u32[]{:S(2)}, u32[]{:S(2)}) collective-permute-start(f32[3,1,450]{2,1,0:T(1,128)} %get-tuple-element.26), channel_id=1, source_target_pairs={{1,0},{2,1},{3,2},{4,3},{5,4},{6,5},{7,6},{8,7},{9,8},{10,9},{11,1... | collective-permute-start | bytes 16208 | tf_op jit(solution)/shard_map/ppermute | solution.py:23
  18.0 16.3 %collective-permute-start.2 = (f32[3,450]{1,0:T(4,128)}, f32[3,450]{1,0:T(4,128)}, u32[]{:S(2)}, u32[]{:S(2)}) collective-permute-start(f32[3,450]{1,0:T(4,128)} %bitcast.95), channel_id=1, source_target_pairs={{0,128},{16,144},{32,160},{48,176},{64,192},{80,208},{96,224},{112... | collective-permute-start | bytes 16208 | tf_op jit(solution)/shard_map/ppermute | solution.py:30
  21.6 12.7 %collective-permute-start.3 = (f32[3,1,450]{2,0,1:T(4,128)}, f32[3,1,450]{2,0,1:T(4,128)}, u32[]{:S(2)}, u32[]{:S(2)}) collective-permute-start(f32[3,1,450]{2,0,1:T(4,128)} %copy.104), channel_id=1, source_target_pairs={{0,1},{1,2},{2,3},{3,4},{4,5},{5,6},{6,7},{7,8},{8,9},{9,10},{10,1... | collective-permute-start | bytes 16208 | tf_op jit(solution)/shard_map/ppermute | solution.py:22
  23.7 6.0 %collective-permute-start = (f32[3,192,1]{2,1,0:T(8,128)S(1)}, f32[3,192,1]{2,1,0:T(8,128)S(1)}, u32[]{:S(2)}, u32[]{:S(2)}) collective-permute-start(f32[3,192,1]{2,1,0:T(8,128)S(1)} %get-tuple-element.29), channel_id=1, source_target_pairs={{16,0},{32,16},{48,32},{64,48},{80,64},{96,80},{112,96},{128,112},... | collective-permute-start | bytes 6920 | tf_op jit(solution)/shard_map/ppermute | solution.py:23
  25.4 8.4 %collective-permute-start.1 = (f32[3,192,1]{2,1,0:T(8,128)S(1)}, f32[3,192,1]{2,1,0:T(8,128)S(1)}, u32[]{:S(2)}, u32[]{:S(2)}) collective-permute-start(f32[3,192,1]{2,1,0:T(8,128)S(1)} %get-tuple-element.30), channel_id=1, source_target_pairs={{0,16},{16,32},{32,48},{48,64},{64,80},{80,96},{96,112},{112,128},... | collective-permute-start | bytes 6920 | tf_op jit(solution)/shard_map/ppermute | solution.py:22
  26.8 9.2 %copy-start.11 = (f32[192]{0:T(256)S(1)}, f32[192]{0:T(256)}, u32[]{:S(2)}) copy-start(f32[192]{0:T(256)} %get-tuple-element.53) | copy-start | bytes 2308
  26.8 9.2 %copy-start.13 = (f32[192]{0:T(256)S(1)}, f32[192]{0:T(256)}, u32[]{:S(2)}) copy-start(f32[192]{0:T(256)} %get-tuple-element.54) | copy-start | bytes 2308
  37.8 8.0 %collective-permute-start.9 = (f32[3,1,450]{2,0,1:T(4,128)S(1)}, f32[3,1,450]{2,0,1:T(4,128)S(1)}, u32[]{:S(2)}, u32[]{:S(2)}) collective-permute-start(f32[3,1,450]{2,0,1:T(4,128)S(1)} %copy.129), channel_id=1, source_target_pairs={{1,0},{2,1},{3,2},{4,3},{5,4},{6,5},{7,6},{8,7},{9,8},{10,9},{11,1... | collective-permute-start | bytes 16208 | tf_op jit(solution)/shard_map/ppermute | solution.py:23
  45.1 67.8 %copy-start.3 = (f32[65,450]{1,0:T(8,128)}, f32[65,450]{1,0:T(8,128)S(1)}, u32[]{:S(2)}) copy-start(f32[65,450]{1,0:T(8,128)S(1)} %get-tuple-element.49) | copy-start | bytes 351004
  45.1 67.8 %copy-start.5 = (f32[65,450]{1,0:T(8,128)}, f32[65,450]{1,0:T(8,128)S(1)}, u32[]{:S(2)}) copy-start(f32[65,450]{1,0:T(8,128)S(1)} %get-tuple-element.50) | copy-start | bytes 351004
  45.1 5.2 %collective-permute-start.7 = (f32[3,450]{1,0:T(4,128)S(1)}, f32[3,450]{1,0:T(4,128)S(1)}, u32[]{:S(2)}, u32[]{:S(2)}) collective-permute-start(f32[3,450]{1,0:T(4,128)S(1)} %bitcast.119), channel_id=1, source_target_pairs={{0,128},{16,144},{32,160},{48,176},{64,192},{80,208},{96,224},{112... | collective-permute-start | bytes 16208 | tf_op jit(solution)/shard_map/ppermute | solution.py:30
  45.8 9.7 %collective-permute-start.8 = (f32[3,1,450]{2,0,1:T(4,128)S(1)}, f32[3,1,450]{2,0,1:T(4,128)S(1)}, u32[]{:S(2)}, u32[]{:S(2)}) collective-permute-start(f32[3,1,450]{2,0,1:T(4,128)S(1)} %get-tuple-element.40), channel_id=1, source_target_pairs={{0,1},{1,2},{2,3},{3,4},{4,5},{5,6},{6,7},{7,8},{8,9},{9,10},{10,1... | collective-permute-start | bytes 16208 | tf_op jit(solution)/shard_map/ppermute | solution.py:22
  47.9 7.8 %collective-permute-start.5 = (f32[3,192,1]{2,1,0:T(8,128)S(1)}, f32[3,192,1]{2,1,0:T(8,128)S(1)}, u32[]{:S(2)}, u32[]{:S(2)}) collective-permute-start(f32[3,192,1]{2,1,0:T(8,128)S(1)} %get-tuple-element.23), channel_id=1, source_target_pairs={{16,0},{32,16},{48,32},{64,48},{80,64},{96,80},{112,96},{128,112},... | collective-permute-start | bytes 6920 | tf_op jit(solution)/shard_map/ppermute | solution.py:23
  48.4 8.8 %collective-permute-start.6 = (f32[3,192,1]{2,1,0:T(8,128)S(1)}, f32[3,192,1]{2,1,0:T(8,128)S(1)}, u32[]{:S(2)}, u32[]{:S(2)}) collective-permute-start(f32[3,192,1]{2,1,0:T(8,128)S(1)} %get-tuple-element.24), channel_id=1, source_target_pairs={{0,16},{16,32},{32,48},{48,64},{64,80},{80,96},{96,112},{112,128},... | collective-permute-start | bytes 6920 | tf_op jit(solution)/shard_map/ppermute | solution.py:22
  62.5 147.7 %all-gather.7.cloned.1.call-start = ((), (), s32[]{:S(2)}) async-start(), calls=%async_computation.1 | async-start | bytes 7102464 | tf_op jit(solution)/shard_map/all_gather | solution.py:59
  62.7 50.2 %copy-start.19 = (pred[192]{0:T(512)(128)(4,1)}, pred[192]{0:T(512)(128)(4,1)S(1)}, u32[]{:S(2)}) copy-start(pred[192]{0:T(512)(128)(4,1)S(1)} %add_compare_fusion) | copy-start | bytes 580
  62.9 50.0 %copy-start.7 = (f32[192,130]{0,1:T(8,128)}, f32[192,130]{0,1:T(8,128)S(1)}, u32[]{:S(2)}) copy-start(f32[192,130]{0,1:T(8,128)S(1)} %pad_maximum_fusion.51) | copy-start | bytes 299524
  115.7 17.3 %copy-start.17 = (f32[3]{0:T(128)S(1)}, f32[3]{0:T(128)}, u32[]{:S(2)}) copy-start(f32[3]{0:T(128)} %constant.58.clone) | copy-start | bytes 40
  115.7 8.0 %collective-permute-start.14 = (f32[3,1,450]{2,0,1:T(4,128)S(1)}, f32[3,1,450]{2,0,1:T(4,128)S(1)}, u32[]{:S(2)}, u32[]{:S(2)}) collective-permute-start(f32[3,1,450]{2,0,1:T(4,128)S(1)} %copy.128), channel_id=1, source_target_pairs={{1,0},{2,1},{3,2},{4,3},{5,4},{6,5},{7,6},{8,7},{9,8},{10,9},{11,1... | collective-permute-start | bytes 16208 | tf_op jit(solution)/shard_map/ppermute | solution.py:23
  121.0 7.2 %collective-permute-start.12 = (f32[3,450]{1,0:T(4,128)S(1)}, f32[3,450]{1,0:T(4,128)S(1)}, u32[]{:S(2)}, u32[]{:S(2)}) collective-permute-start(f32[3,450]{1,0:T(4,128)S(1)} %bitcast.121), channel_id=1, source_target_pairs={{0,128},{16,144},{32,160},{48,176},{64,192},{80,208},{96,224},{112... | collective-permute-start | bytes 16208 | tf_op jit(solution)/shard_map/ppermute | solution.py:30
  123.7 9.3 %collective-permute-start.13 = (f32[3,1,450]{2,0,1:T(4,128)S(1)}, f32[3,1,450]{2,0,1:T(4,128)S(1)}, u32[]{:S(2)}, u32[]{:S(2)}) collective-permute-start(f32[3,1,450]{2,0,1:T(4,128)S(1)} %get-tuple-element.36), channel_id=1, source_target_pairs={{0,1},{1,2},{2,3},{3,4},{4,5},{5,6},{6,7},{7,8},{8,9},{9,10},{10,1... | collective-permute-start | bytes 16208 | tf_op jit(solution)/shard_map/ppermute | solution.py:22
  125.8 7.4 %collective-permute-start.10 = (f32[3,192,1]{2,1,0:T(8,128)S(1)}, f32[3,192,1]{2,1,0:T(8,128)S(1)}, u32[]{:S(2)}, u32[]{:S(2)}) collective-permute-start(f32[3,192,1]{2,1,0:T(8,128)S(1)} %get-tuple-element.19), channel_id=1, source_target_pairs={{16,0},{32,16},{48,32},{64,48},{80,64},{96,80},{112,96},{128,112},... | collective-permute-start | bytes 6920 | tf_op jit(solution)/shard_map/ppermute | solution.py:23
  128.2 8.3 %collective-permute-start.11 = (f32[3,192,1]{2,1,0:T(8,128)S(1)}, f32[3,192,1]{2,1,0:T(8,128)S(1)}, u32[]{:S(2)}, u32[]{:S(2)}) collective-permute-start(f32[3,192,1]{2,1,0:T(8,128)S(1)} %get-tuple-element.20), channel_id=1, source_target_pairs={{0,16},{16,32},{32,48},{48,64},{64,80},{80,96},{96,112},{112,128},... | collective-permute-start | bytes 6920 | tf_op jit(solution)/shard_map/ppermute | solution.py:22
  139.1 8.0 %collective-permute-start.19 = (f32[3,1,450]{2,0,1:T(4,128)S(1)}, f32[3,1,450]{2,0,1:T(4,128)S(1)}, u32[]{:S(2)}, u32[]{:S(2)}) collective-permute-start(f32[3,1,450]{2,0,1:T(4,128)S(1)} %copy.127), channel_id=1, source_target_pairs={{1,0},{2,1},{3,2},{4,3},{5,4},{6,5},{7,6},{8,7},{9,8},{10,9},{11,1... | collective-permute-start | bytes 16208 | tf_op jit(solution)/shard_map/ppermute | solution.py:23
  145.7 5.2 %collective-permute-start.17 = (f32[3,450]{1,0:T(4,128)S(1)}, f32[3,450]{1,0:T(4,128)S(1)}, u32[]{:S(2)}, u32[]{:S(2)}) collective-permute-start(f32[3,450]{1,0:T(4,128)S(1)} %bitcast.120), channel_id=1, source_target_pairs={{0,128},{16,144},{32,160},{48,176},{64,192},{80,208},{96,224},{112... | collective-permute-start | bytes 16208 | tf_op jit(solution)/shard_map/ppermute | solution.py:30
  147.1 9.4 %collective-permute-start.18 = (f32[3,1,450]{2,0,1:T(4,128)S(1)}, f32[3,1,450]{2,0,1:T(4,128)S(1)}, u32[]{:S(2)}, u32[]{:S(2)}) collective-permute-start(f32[3,1,450]{2,0,1:T(4,128)S(1)} %get-tuple-element.32), channel_id=1, source_target_pairs={{0,1},{1,2},{2,3},{3,4},{4,5},{5,6},{6,7},{7,8},{8,9},{9,10},{10,1... | collective-permute-start | bytes 16208 | tf_op jit(solution)/shard_map/ppermute | solution.py:22
  149.1 7.5 %collective-permute-start.15 = (f32[3,192,1]{2,1,0:T(8,128)S(1)}, f32[3,192,1]{2,1,0:T(8,128)S(1)}, u32[]{:S(2)}, u32[]{:S(2)}) collective-permute-start(f32[3,192,1]{2,1,0:T(8,128)S(1)} %get-tuple-element.15), channel_id=1, source_target_pairs={{16,0},{32,16},{48,32},{64,48},{80,64},{96,80},{112,96},{128,112},... | collective-permute-start | bytes 6920 | tf_op jit(solution)/shard_map/ppermute | solution.py:23
  149.2 8.7 %collective-permute-start.16 = (f32[3,192,1]{2,1,0:T(8,128)S(1)}, f32[3,192,1]{2,1,0:T(8,128)S(1)}, u32[]{:S(2)}, u32[]{:S(2)}) collective-permute-start(f32[3,192,1]{2,1,0:T(8,128)S(1)} %get-tuple-element.16), channel_id=1, source_target_pairs={{0,16},{16,32},{32,48},{48,64},{64,80},{80,96},{96,112},{112,128},... | collective-permute-start | bytes 6920 | tf_op jit(solution)/shard_map/ppermute | solution.py:22
  (11 other events, 27.7 us)
Sparse Core Ops, SparseCore 0:
  62.6 46.9 all-gather.4
  162.8 47.2 all-gather.6
